TPU v7x, 32 devices: a whole 2x2x4 slice. The times are simulated.
32 devices in a mesh: pair: 8 (over z, core), orb: 4 (over y, x).
Axes of the slice: x: 2, y: 2, z: 4, core: 2. Of those that a mesh axis runs over, the one named last changes fastest.
Arguments:
- amplitudes: bfloat16 [8, 2, 600, 600], P('pair', None, 'orb'), may hold values from -6 to 6
- factors: bfloat16 [48, 360000], P('orb', 'pair'), may hold values from -0.21875 to 0.21875
- crossed_amplitudes: bfloat16 [8, 64, 600, 600], P('pair', None, 'orb'), may hold values from -6 to 6
- crossed_coupling: bfloat16 [38400, 1200], P('orb', 'pair'), may hold values from -0.03125 to 0.03125
Outputs:
- residual: float32 [8, 600, 2, 600], P('pair', 'orb')
All inputs are finite; a program needn't handle non-finite values.
Results may differ from a plain program's by a relative error of at most 0.0023.
Values may be sent and summed in bfloat16 or wider, within the bound.
No kernel may reach another device: no remote copies, remote signals or barrier semaphores. Data moves between devices by JAX's collectives and lax.ppermute only.
A program may use at most 256 MiB of HBM per device.

v0:
```python
import jax
import jax.numpy as jnp
from jax import lax
from jax.sharding import PartitionSpec as P

NV = 600


def ladder_term(amplitudes, factors, nvirt):
    pair_amps = lax.all_gather(amplitudes, "orb", axis=2, tiled=True)
    factor_rows = lax.all_gather(factors, "pair", axis=1, tiled=True)
    cube = factor_rows.reshape(factor_rows.shape[0], nvirt, nvirt)
    inner = jnp.einsum(
        "qac,jcd->jqad", cube, pair_amps[0], preferred_element_type=jnp.float32
    ).astype(jnp.bfloat16)
    return jnp.einsum("jqad,qbd->ajb", inner, cube, preferred_element_type=jnp.float32)


def crossed_term(crossed_amplitudes, crossed_coupling, nvirt):
    relaid = lax.all_to_all(crossed_amplitudes[0], "orb", split_axis=0, concat_axis=1, tiled=True)
    k_local = relaid.shape[0]
    piece = lax.all_gather(crossed_coupling, "pair", axis=1, tiled=True)
    block = piece.reshape(k_local, nvirt, piece.shape[1])
    product = jnp.einsum("kac,kcn->an", relaid, block, preferred_element_type=jnp.float32)
    return product.reshape(nvirt, product.shape[1] // nvirt, nvirt)


def on_device(amplitudes, factors, crossed_amplitudes, crossed_coupling):
    nvirt = NV
    ladder = ladder_term(amplitudes, factors, nvirt)
    crossed = crossed_term(crossed_amplitudes, crossed_coupling, nvirt)
    total = lax.psum_scatter(ladder, "orb", scatter_dimension=0, tiled=True) + lax.psum_scatter(
        crossed, "orb", scatter_dimension=0, tiled=True
    )
    return total[None]


def solution(mesh):
    return jax.shard_map(
        on_device,
        mesh=mesh,
        in_specs=(
            P("pair", None, "orb", None),
            P("orb", "pair"),
            P("pair", None, "orb", None),
            P("orb", "pair"),
        ),
        out_specs=P("pair", "orb", None, None),
        check_vma=False,
    )
```

profile of v0, /device:TPU:0, one launch (start us, length us, event | category | flops | bytes accessed | tf_op | source)
XLA Modules:
  0.0 646.5 jit_solution(15938430260463364513)
XLA Ops:
  6.5 0.0 all-gather.6.cloned.1.call-start
  6.5 0.7 all-gather.6.cloned.1.call-update
  7.3 0.0 all-gather.8.cloned.1.call-start
  7.3 0.7 all-gather.8.cloned.1.call-update
  8.0 0.0 all-gather.10.cloned.1.call-start
  8.1 0.7 all-gather.10.cloned.1.call-update
  8.7 14.3 %copy.40 = bf16[1,64,150,600]{3,2,1,0:T(8,128)(2,1)} copy(bf16[1,64,150,600]{3,1,2,0:T(8,128)(2,1)} %param.6) | data formatting | bytes 23040000 | tf_op args[2]
  23.1 6.4 all-to-all-start
  29.4 0.3 all-reduce.3.cloned.1.call-start
  29.7 87.7 %all-gather.6.cloned.1.call-done = bf16[1,2,600,600]{3,1,0,2:T(2,128)(2,1)} async-done(((bf16[1,2,150,600]{3,1,0,2:T(2,128)(2,1)}), bf16[1,2,600,600]{3,1,0,2:T(2,128)(2,1)}) %all-gather.6.cloned.1.call-update) | async-done | bytes 1440016 | tf_op jit(solution)/shard_map/all_gather | solution.py:10
  117.4 3.8 copy.19
  121.2 53.8 %all-to-all-done = bf16[64,150,600]{2,1,0:T(8,128)(2,1)} async-done(((bf16[64,150,600]{2,1,0:T(8,128)(2,1)}), bf16[64,150,600]{2,1,0:T(8,128)(2,1)}, u32[]{:S(2)}, u32[]{:S(2)}) %all-to-all-start) | async-done | bytes 11520032 | tf_op jit(solution)/shard_map/all_to_all | solution.py:20
  175.0 27.9 %copy.24 = bf16[16,4,150,600]{3,0,2,1:T(8,128)(2,1)} copy(bf16[16,4,150,600]{3,2,0,1:T(8,128)(2,1)} %bitcast.14) | data formatting | bytes 23040000 | tf_op jit(solution)/shard_map/all_to_all | solution.py:20
  202.9 23.4 %all-gather.8.cloned.1.call-done = bf16[8,45000,12]{1,2,0:T(8,128)(2,1)} async-done(((bf16[1,45000,12]{1,2,0:T(8,128)(2,1)}), bf16[8,45000,12]{1,2,0:T(8,128)(2,1)}) %all-gather.8.cloned.1.call-update) | async-done | bytes 8640016 | tf_op jit(solution)/shard_map/all_gather | solution.py:11
  226.4 13.7 %copy.20 = bf16[8,45000,12]{1,0,2:T(8,128)(2,1)} copy(bf16[8,45000,12]{1,2,0:T(8,128)(2,1)} %all-gather.8.cloned.1.call-done) | data formatting | bytes 17280000 | tf_op jit(solution)/shard_map/all_gather | solution.py:11
  240.1 34.1 %reshape.11 = bf16[360000,12]{0,1:T(8,128)(2,1)} reshape(bf16[8,45000,12]{1,0,2:T(8,128)(2,1)} %copy.20) | data formatting | bytes 17280000
  274.2 23.4 %reshape.15 = bf16[12,600,600,1]{2,1,0,3:T(8,128)(2,1)} reshape(bf16[12,360000]{1,0:T(8,128)(2,1)} %bitcast.66) | data formatting | bytes 17280000 | tf_op jit(solution)/shard_map/reshape | solution.py:12
  297.7 21.1 %fusion.24 = bf16[2,12,600,600]{2,3,1,0:T(8,128)(2,1)} fusion(bf16[12,600,600,1]{2,1,0,3:T(8,128)(2,1)} %reshape.15, bf16[1,2,600,600]{2,3,1,0:T(8,128)(2,1)S(1)} %copy.19), kind=kOutput, calls=%fused_computation.3.clone.clone.clone.1 | convolution fusion | flops 10376640512 | bytes 27360000 | tf_op jit(solution)/shard_map/qac,jcd->jqad/dot_general | solution.py:13
  318.8 112.4 %all-gather.10.cloned.1.call-done = bf16[8,150,9600]{2,1,0:T(8,128)(2,1)} async-done(((bf16[1,150,9600]{2,1,0:T(8,128)(2,1)}), bf16[8,150,9600]{2,1,0:T(8,128)(2,1)}) %all-gather.10.cloned.1.call-update) | async-done | bytes 23040016 | tf_op jit(solution)/shard_map/all_gather | solution.py:22
  431.2 24.2 %reshape.13 = bf16[1200,9600]{1,0:T(8,128)(2,1)} reshape(bf16[8,150,9600]{2,1,0:T(8,128)(2,1)} %all-gather.10.cloned.1.call-done) | data formatting | bytes 46080000
  455.4 49.1 %reshape.9 = bf16[16,600,1200]{1,0,2:T(8,128)(2,1)} reshape(bf16[9600,1200]{0,1:T(8,128)(2,1)} %bitcast.64) | data formatting | bytes 46080000 | tf_op jit(solution)/shard_map/reshape | solution.py:23
  504.5 24.8 %fusion = f32[600,2,600,1]{2,0,3,1:T(8,128)S(1)} fusion(bf16[2,600,600,16]{2,3,1,0:T(8,128)(2,1)} %bitcast.67, bf16[16,600,600]{2,0,1:T(8,128)(2,1)} %bitcast.68), kind=kOutput, calls=%fused_computation | convolution fusion | flops 13824000000 | bytes 37440000 | tf_op jit(solution)/shard_map/kac,kcn->an/dot_general | solution.py:24
  529.3 20.6 %bitcast_add_fusion = f32[600,2,600]{2,0,1:T(8,128)S(1)} fusion(f32[600,2,600,1]{2,0,3,1:T(8,128)S(1)} %fusion, bf16[12,600,600,1]{2,1,0,3:T(8,128)(2,1)} %reshape.15, bf16[2,12,600,600]{2,3,1,0:T(8,128)(2,1)} %fusion.24), kind=kOutput, calls=%fused_computation.8 | convolution fusion | flops 10368719872 | bytes 31680000 | tf_op jit(solution)/shard_map/jqad,qbd->ajb/dot_general | solution.py:16
  549.9 0.0 copy-start
  549.9 3.2 copy.27
  553.1 0.0 all-reduce.3.cloned.1.call-update
  553.1 0.0 copy-done
  553.1 0.6 dynamic-slice
  554.4 82.9 %all-reduce.3.cloned.1.call-done = f32[600,2,600]{2,1,0:T(2,128)} async-done(((f32[600,2,600]{2,1,0:T(2,128)}), f32[600,2,600]{2,1,0:T(2,128)}) %all-reduce.3.cloned.1.call-update) | async-done | bytes 2880016
  637.2 2.3 dynamic-slice_bitcast_fusion
Async XLA Ops:
  6.5 110.9 %all-gather.6.cloned.1.call-start = ((), (), s32[]{:S(2)}) async-start(), calls=%async_computation.1 | async-start | bytes 1920000 | tf_op jit(solution)/shard_map/all_gather | solution.py:10
  7.3 219.1 %all-gather.8.cloned.1.call-start = ((), (), s32[]{:S(2)}) async-start(), calls=%async_computation.2 | async-start | bytes 12976128 | tf_op jit(solution)/shard_map/all_gather | solution.py:11
  8.0 423.2 %all-gather.10.cloned.1.call-start = ((), (), s32[]{:S(2)}) async-start(), calls=%async_computation.3 | async-start | bytes 26265600 | tf_op jit(solution)/shard_map/all_gather | solution.py:22
  23.1 151.9 %all-to-all-start = ((bf16[64,150,600]{2,1,0:T(8,128)(2,1)}), bf16[64,150,600]{2,1,0:T(8,128)(2,1)}, u32[]{:S(2)}, u32[]{:S(2)}) async-start(bf16[64,150,600]{2,1,0:T(8,128)(2,1)} %bitcast.65), calls=%async_computation | async-start | bytes 24903680 | tf_op jit(solution)/shard_map/all_to_all | solution.py:20
  29.4 607.8 %all-reduce.3.cloned.1.call-start = ((), (), s32[]{:S(2)}) async-start(), calls=%async_computation.4 | async-start | bytes 6144000
  549.9 3.3 copy-start
Sparse Core Ops, SparseCore 0:
  9.2 108.2 all-gather.5
  119.1 107.2 all-gather.7
  228.0 203.1 all-gather.9
  553.2 83.9 all-reduce.2
where the time goes:
time: 651 us; the launch traced here: 646 us
  waiting for transfers between devices  362 us (56%)
  local copies, waits for them, and re-layouts  197 us (30%)
  matrix products  66.5 us (10%)
  between operations  14.3 us (2%)
  starting transfers between devices  6.7 us (1%)
    all_gather x1, waiting for transfers between devices, crossed_term(): piece = lax.all_gather(crossed_coupling, 'pair', axis=1, tiled=True)  112 us
    all_gather x1, waiting for transfers between devices, ladder_term(): pair_amps = lax.all_gather(amplitudes, 'orb', axis=2, tiled=True)  87.7 us
    unnamed x5, waiting for transfers between devices  85 us
    unnamed x6, local copies, waits for them, and re-layouts  73.2 us
    all_to_all x1, waiting for transfers between devices, crossed_term(): lax.all_to_all(crossed_amplitudes[0], 'orb', split_axis=0, concat_axis=1,...  53.8 us
    reshape x1, local copies, waits for them, and re-layouts, crossed_term(): block = piece.reshape(k_local, nvirt, piece.shape[1])  49.1 us
    all_to_all x1, local copies, waits for them, and re-layouts, crossed_term(): lax.all_to_all(crossed_amplitudes[0], 'orb', split_axis=0, concat_axis=1,...  27.9 us
    dot_general x1, matrix products, crossed_term(): jnp.einsum('kac,kcn->an', relaid, block, preferred_element_type=jnp.float32)  24.8 us
  transfers between devices with their start and end apart: 5, of which 5 were waited for; matrix products, arithmetic and copies ran while one was open for 22% of the time, Pallas kernels for 0%

commit v1 on v0

--- a/solution.py
+++ b/solution.py
@@ -7,7 +7,15 @@
 
 
 def ladder_term(amplitudes, factors, nvirt):
-    pair_amps = lax.all_gather(amplitudes, "orb", axis=2, tiled=True)
+    ways, here = (lax.axis_size("orb"), lax.axis_index("orb"))
+    grown, reach = (amplitudes, 1)
+    while reach < ways:
+        theirs = lax.ppermute(grown, "orb", [(d, d ^ reach) for d in range(ways)])
+        mine_first = jnp.concatenate([grown, theirs], axis=2)
+        theirs_first = jnp.concatenate([theirs, grown], axis=2)
+        grown = jnp.where(here & reach == 0, mine_first, theirs_first)
+        reach = 2 * reach
+    pair_amps = grown
     factor_rows = lax.all_gather(factors, "pair", axis=1, tiled=True)
     cube = factor_rows.reshape(factor_rows.shape[0], nvirt, nvirt)
     inner = jnp.einsum(

time: 651 us -> 544 us (0.84)
  waiting for transfers between devices: 362 us -> 242 us
  other arithmetic: 0 us -> 15.2 us
    ppermute x0 -> x2, waiting for transfers between devices: none -> 155 us  [ladder_term(): theirs = lax.ppermute(grown, 'orb', [(d, d ^ reach) for d in range(ways)])]
    all_gather x1, waiting for transfers between devices: 112 us -> 2.65 us  [crossed_term(): piece = lax.all_gather(crossed_coupling, 'pair', axis=1, tiled=True)]
    all_gather x1 -> x0, waiting for transfers between devices: 87.7 us -> none  [ladder_term(): pair_amps = lax.all_gather(amplitudes, 'orb', axis=2, tiled=True)]
    all_to_all x1, waiting for transfers between devices: 53.8 us -> 0.01 us  [crossed_term(): lax.all_to_all(crossed_amplitudes[0], 'orb', split_axis=0, concat_axis=1,...]
    all_gather x1, waiting for transfers between devices: 23.4 us -> 0.02 us  [ladder_term(): factor_rows = lax.all_gather(factors, 'pair', axis=1, tiled=True)]
    select_n x0 -> x3, other arithmetic: none -> 15.2 us  [ladder_term(): grown = jnp.where(here & reach == 0, mine_first, theirs_first)]
    unnamed x5 -> x4, waiting for transfers between devices: 85 us -> 84.3 us
    unnamed x6 -> x8, local copies, waits for them, and re-layouts: 73.2 us -> 72.6 us
  transfers between devices with their start and end apart: 5 -> 6, of which waited for: 5 -> 4; matrix products, arithmetic and copies ran while one was open for 22% -> 27% of each run, Pallas kernels for 0% -> 0%
where the time goes in v1:
time: 544 us; the launch traced here: 540 us
  waiting for transfers between devices  242 us (44%)
  local copies, waits for them, and re-layouts  191 us (35%)
  matrix products  65.3 us (12%)
  other arithmetic  15.2 us (3%)
  between operations  14.3 us (3%)
  starting transfers between devices  11.3 us (2%)
    ppermute x2, waiting for transfers between devices, ladder_term(): theirs = lax.ppermute(grown, 'orb', [(d, d ^ reach) for d in range(ways)])  155 us
    unnamed x4, waiting for transfers between devices  84.3 us
    unnamed x8, local copies, waits for them, and re-layouts  72.6 us
    reshape x1, local copies, waits for them, and re-layouts, crossed_term(): block = piece.reshape(k_local, nvirt, piece.shape[1])  49.1 us
    all_to_all x1, local copies, waits for them, and re-layouts, crossed_term(): lax.all_to_all(crossed_amplitudes[0], 'orb', split_axis=0, concat_axis=1,...  28.5 us
    dot_general x1, matrix products, crossed_term(): jnp.einsum('kac,kcn->an', relaid, block, preferred_element_type=jnp.float32)  24.8 us
    reshape x1, local copies, waits for them, and re-layouts, ladder_term(): cube = factor_rows.reshape(factor_rows.shape[0], nvirt, nvirt)  23.2 us
    dot_general x1, matrix products, ladder_term(): jnp.einsum('jqad,qbd->ajb', inner, cube, preferred_element_type=jnp.float32)  20.6 us
  transfers between devices with their start and end apart: 6, of which 4 were waited for; matrix products, arithmetic and copies ran while one was open for 27% of the time, Pallas kernels for 0%

profile of v1, /device:TPU:0, one launch (start us, length us, event | category | flops | bytes accessed | tf_op | source)
XLA Modules:
  0.0 539.9 jit_solution(15371621985668945203)
XLA Ops:
  6.5 0.0 all-gather.5.cloned.1.call-start
  6.5 0.7 all-gather.5.cloned.1.call-update
  7.3 0.0 all-gather.7.cloned.1.call-start
  7.3 0.7 all-gather.7.cloned.1.call-update
  8.0 14.4 %copy.47 = bf16[1,64,150,600]{3,2,1,0:T(8,128)(2,1)} copy(bf16[1,64,150,600]{3,1,2,0:T(8,128)(2,1)} %param.6) | data formatting | bytes 23040000 | tf_op args[2]
  22.4 0.0 copy-start
  22.4 6.5 %all-to-all-start = ((bf16[64,150,600]{2,1,0:T(8,128)(2,1)}), bf16[64,150,600]{2,1,0:T(8,128)(2,1)}, u32[]{:S(2)}, u32[]{:S(2)}) async-start(bf16[64,150,600]{2,1,0:T(8,128)(2,1)} %bitcast.59), calls=%async_computation | async-start | bytes 24903680 | tf_op jit(solution)/shard_map/all_to_all | solution.py:28
  28.9 0.3 all-reduce.3.cloned.1.call-start
  29.2 0.0 copy-done
  29.2 3.0 collective-permute-start
  32.2 142.2 %collective-permute-done = bf16[1,2,150,600]{3,1,2,0:T(2,128)(2,1)S(1)} collective-permute-done((bf16[1,2,150,600]{3,1,2,0:T(2,128)(2,1)S(1)}, bf16[1,2,150,600]{3,1,2,0:T(2,128)(2,1)S(1)}, u32[]{:S(2)}, u32[]{:S(2)}) %collective-permute-start) | collective-permute-done | bytes 360032 | tf_op jit(solution)/shard_map/ppermute | solution.py:13
  174.4 3.8 broadcast_select_fusion.1
  178.2 1.5 collective-permute-start.1
  179.7 3.8 broadcast_select_fusion.2
  183.6 13.1 %collective-permute-done.1 = bf16[1,2,300,600]{3,1,2,0:T(2,128)(2,1)S(1)} collective-permute-done((bf16[1,2,300,600]{3,1,2,0:T(2,128)(2,1)S(1)}, bf16[1,2,300,600]{3,1,2,0:T(2,128)(2,1)S(1)}, u32[]{:S(2)}, u32[]{:S(2)}) %collective-permute-start.1) | collective-permute-done | bytes 720032 | tf_op jit(solution)/shard_map/ppermute | solution.py:13
  196.7 7.6 %fusion.11 = bf16[2,600,600,1]{2,0,1,3:T(2,128)(2,1)S(1)} fusion(pred[]{:T(512)S(6)} %eq.6, bf16[2,300,600]{2,0,1:T(2,128)(2,1)S(1)} %bitcast.67, bf16[2,300,600]{2,0,1:T(2,128)(2,1)S(1)} %broadcast_select_fusion.2), kind=kLoop, calls=%fused_computation.11 | loop fusion | flops 2160000 | bytes 2880001 | tf_op jit(solution)/shard_map/jit(_where)/select_n | solution.py:16
  204.3 0.0 all-to-all-done
  204.3 28.5 %copy.23 = bf16[16,4,150,600]{3,0,2,1:T(8,128)(2,1)} copy(bf16[16,4,150,600]{3,2,0,1:T(8,128)(2,1)} %bitcast.14) | data formatting | bytes 23040000 | tf_op jit(solution)/shard_map/all_to_all | solution.py:28
  232.8 0.0 all-gather.5.cloned.1.call-done
  232.8 12.6 %copy.18 = bf16[8,45000,12]{1,0,2:T(8,128)(2,1)} copy(bf16[8,45000,12]{1,2,0:T(8,128)(2,1)} %all-gather.5.cloned.1.call-done) | data formatting | bytes 17280000 | tf_op jit(solution)/shard_map/all_gather | solution.py:19
  245.3 33.4 %reshape.94 = bf16[360000,12]{0,1:T(8,128)(2,1)} reshape(bf16[8,45000,12]{1,0,2:T(8,128)(2,1)} %copy.18) | data formatting | bytes 17280000
  278.8 23.2 %reshape.98 = bf16[12,600,600,1]{2,1,0,3:T(8,128)(2,1)} reshape(bf16[12,360000]{1,0:T(8,128)(2,1)} %bitcast.60) | data formatting | bytes 17280000 | tf_op jit(solution)/shard_map/reshape | solution.py:20
  302.0 20.0 %fusion.25 = bf16[2,12,600,600]{2,3,1,0:T(8,128)(2,1)} fusion(bf16[12,600,600,1]{2,1,0,3:T(8,128)(2,1)} %reshape.98, bf16[2,600,600,1]{2,0,1,3:T(2,128)(2,1)S(1)} %fusion.11), kind=kOutput, calls=%fused_computation.3.clone.clone.clone.1 | convolution fusion | flops 10376640512 | bytes 27360000 | tf_op jit(solution)/shard_map/qac,jcd->jqad/dot_general | solution.py:21
  322.0 2.7 all-gather.7.cloned.1.call-done
  324.6 24.2 %reshape.96 = bf16[1200,9600]{1,0:T(8,128)(2,1)} reshape(bf16[8,150,9600]{2,1,0:T(8,128)(2,1)} %all-gather.7.cloned.1.call-done) | data formatting | bytes 46080000
  348.8 49.1 %reshape.92 = bf16[16,600,1200]{1,0,2:T(8,128)(2,1)} reshape(bf16[9600,1200]{0,1:T(8,128)(2,1)} %bitcast.58) | data formatting | bytes 46080000 | tf_op jit(solution)/shard_map/reshape | solution.py:31
  397.9 24.8 %fusion = f32[600,2,600,1]{2,0,3,1:T(8,128)S(1)} fusion(bf16[2,600,600,16]{2,3,1,0:T(8,128)(2,1)} %bitcast.61, bf16[16,600,600]{2,0,1:T(8,128)(2,1)} %bitcast.62), kind=kOutput, calls=%fused_computation | convolution fusion | flops 13824000000 | bytes 37440000 | tf_op jit(solution)/shard_map/kac,kcn->an/dot_general | solution.py:32
  422.7 20.6 %bitcast_add_fusion = f32[600,2,600]{2,0,1:T(8,128)S(1)} fusion(f32[600,2,600,1]{2,0,3,1:T(8,128)S(1)} %fusion, bf16[12,600,600,1]{2,1,0,3:T(8,128)(2,1)} %reshape.98, bf16[2,12,600,600]{2,3,1,0:T(8,128)(2,1)} %fusion.25), kind=kOutput, calls=%fused_computation.8 | convolution fusion | flops 10368719872 | bytes 31680000 | tf_op jit(solution)/shard_map/jqad,qbd->ajb/dot_general | solution.py:24
  443.3 0.0 copy-start.1
  443.3 3.2 copy.26
  446.5 0.0 all-reduce.3.cloned.1.call-update
  446.5 0.0 copy-done.1
  446.6 0.6 dynamic-slice
  447.8 82.9 %all-reduce.3.cloned.1.call-done = f32[600,2,600]{2,1,0:T(2,128)} async-done(((f32[600,2,600]{2,1,0:T(2,128)}), f32[600,2,600]{2,1,0:T(2,128)}) %all-reduce.3.cloned.1.call-update) | async-done | bytes 2880016
  530.7 2.3 dynamic-slice_bitcast_fusion
Async XLA Ops:
  6.5 226.2 %all-gather.5.cloned.1.call-start = ((), (), s32[]{:S(2)}) async-start(), calls=%async_computation.1 | async-start | bytes 12976128 | tf_op jit(solution)/shard_map/all_gather | solution.py:19
  7.3 317.4 %all-gather.7.cloned.1.call-start = ((), (), s32[]{:S(2)}) async-start(), calls=%async_computation.2 | async-start | bytes 26265600 | tf_op jit(solution)/shard_map/all_gather | solution.py:30
  22.4 6.8 %copy-start = (bf16[1,2,150,600]{3,1,2,0:T(2,128)(2,1)S(1)}, bf16[1,2,150,600]{3,1,2,0:T(2,128)(2,1)}, u32[]{:S(2)}) copy-start(bf16[1,2,150,600]{3,1,2,0:T(2,128)(2,1)} %param.4) | copy-start | bytes 1080004
  22.4 181.9 %all-to-all-start = ((bf16[64,150,600]{2,1,0:T(8,128)(2,1)}), bf16[64,150,600]{2,1,0:T(8,128)(2,1)}, u32[]{:S(2)}, u32[]{:S(2)}) async-start(bf16[64,150,600]{2,1,0:T(8,128)(2,1)} %bitcast.59), calls=%async_computation | async-start | bytes 24903680 | tf_op jit(solution)/shard_map/all_to_all | solution.py:28
  28.9 501.8 %all-reduce.3.cloned.1.call-start = ((), (), s32[]{:S(2)}) async-start(), calls=%async_computation.3 | async-start | bytes 6144000
  29.2 145.2 %collective-permute-start = (bf16[1,2,150,600]{3,1,2,0:T(2,128)(2,1)S(1)}, bf16[1,2,150,600]{3,1,2,0:T(2,128)(2,1)S(1)}, u32[]{:S(2)}, u32[]{:S(2)}) collective-permute-start(bf16[1,2,150,600]{3,1,2,0:T(2,128)(2,1)S(1)} %copy-done), channel_id=1, source_target_pairs={{0,1},{1,0},{2,3},{3,2},{4,5},{5,4},{6,7},{7,6},{8,9},{9,8},{10,11... | collective-permute-start | bytes 1080008 | tf_op jit(solution)/shard_map/ppermute | solution.py:13
  178.2 18.5 %collective-permute-start.1 = (bf16[1,2,300,600]{3,1,2,0:T(2,128)(2,1)S(1)}, bf16[1,2,300,600]{3,1,2,0:T(2,128)(2,1)S(1)}, u32[]{:S(2)}, u32[]{:S(2)}) collective-permute-start(bf16[1,2,300,600]{3,1,2,0:T(2,128)(2,1)S(1)} %broadcast_select_fusion.1), channel_id=1, source_target_pairs={{0,2},{1,3},{2,0},{3,1},{4,6},{5,7},{6,4},{7,5},{8,10},{9,11},{10,... | collective-permute-start | bytes 2160008 | tf_op jit(solution)/shard_map/ppermute | solution.py:13
  443.3 3.3 copy-start.1
Sparse Core Ops, SparseCore 0:
  9.0 110.7 all-gather.4
  121.4 203.1 all-gather.6
  446.7 83.9 all-reduce.2
